TPU v7x, 32 devices: a whole 2x2x4 slice. The times are simulated.
32 devices in a mesh: section: 8 (over z, core), seq: 4 (over y, x).
Axes of the slice: x: 2, y: 2, z: 4, core: 2. Of those that a mesh axis runs over, the one named last changes fastest.
Arguments:
- queries: bfloat16 [8, 512, 8192], P('section', 'seq'), may hold values from -48 to 48
- key_states: bfloat16 [8, 512, 1024], P('section', 'seq'), may hold values from -6 to 6
- section_value_states: bfloat16 [8, 512, 1024], P('section', 'seq'), may hold values from -6 to 6
- out_grad: bfloat16 [8, 512, 8192], P('section', 'seq'), may hold values from -1.5 to 1.5
- layer_input: bfloat16 [8, 512, 8192], P('section', 'seq'), may hold values from -6 to 6
- doc_segments: int32 [8, 512], P('section', 'seq'), may hold values from 0 to 3, never falling along the last dimension, each value on 1 to 256 neighbouring positions
Outputs:
- query_grad: bfloat16 [8, 512, 8192], P('section', 'seq')
- key_grad: bfloat16 [8, 512, 1024], P('section', 'seq')
- weight_grad: bfloat16 [8, 8192, 1024], P('section', None, 'seq')
Inputs may be any that keep to these rules, and one draw needn't show every extreme that they name: `doc_segments`: document numbers never fall along a section's positions; a document holds at most 256 positions.
All inputs are finite; a program needn't handle non-finite values.
Results may differ from a plain program's by a relative error of at most 0.012.
The roundings to bfloat16 on the way count: a program that leaves them out, or rounds other values in their place, can miss the bound.
Values may be sent and summed in bfloat16 or wider, within the bound.
No kernel may reach another device: no remote copies, remote signals or barrier semaphores. Data moves between devices by JAX's collectives and lax.ppermute only.
A program may use at most 128 MiB of HBM per device.

v0:
```python
import math

import jax
import jax.numpy as jnp
from jax import lax
from jax.sharding import PartitionSpec as P

HEAD_WIDTH = 128


def group_pass(query_group, key_col, value_col, grad_group, allowed):
    scale_factor = 1.0 / math.sqrt(key_col.shape[1])

    def one_head(totals, head_inputs):
        query_one, grad_one = head_inputs
        key_acc, value_acc = totals
        scores = jnp.dot(query_one, key_col.T, preferred_element_type=jnp.float32) * scale_factor
        scores = jnp.where(allowed, scores, -jnp.inf)
        row_max = jnp.max(scores, axis=1, keepdims=True)
        weights = jnp.exp(scores - row_max)
        attention = weights / jnp.sum(weights, axis=1, keepdims=True)
        probs_low = attention.astype(jnp.bfloat16)
        attended = jnp.dot(probs_low, value_col, preferred_element_type=jnp.float32).astype(
            jnp.bfloat16
        )
        attended = lax.optimization_barrier(attended)
        row_delta = jnp.sum(
            grad_one.astype(jnp.float32) * attended.astype(jnp.float32), axis=1, keepdims=True
        )
        dprobs = jnp.dot(grad_one, value_col.T, preferred_element_type=jnp.float32)
        dscores = (attention * (dprobs - row_delta) * scale_factor).astype(jnp.bfloat16)
        query_part = jnp.dot(dscores, key_col, preferred_element_type=jnp.float32).astype(
            jnp.bfloat16
        )
        key_acc = key_acc + jnp.dot(dscores.T, query_one, preferred_element_type=jnp.float32)
        value_acc = value_acc + jnp.dot(probs_low.T, grad_one, preferred_element_type=jnp.float32)
        return ((key_acc, value_acc), query_part)

    starting = jnp.zeros(key_col.shape, jnp.float32)
    (key_acc, value_acc), query_parts = lax.scan(
        one_head, (starting, starting), (query_group, grad_group)
    )
    return (query_parts, key_acc.astype(jnp.bfloat16), value_acc.astype(jnp.bfloat16))


def attention_grads(query_cols, key_cols, value_cols, grad_cols, doc_ids):
    length = query_cols.shape[0]
    kv_heads = key_cols.shape[1] // HEAD_WIDTH
    q_heads = query_cols.shape[1] // HEAD_WIDTH
    group_size = q_heads // kv_heads
    position = jnp.arange(length, dtype=jnp.int32)
    allowed = (position[:, None] >= position[None, :]) & (doc_ids[:, None] == doc_ids[None, :])
    query_split = query_cols.reshape(length, kv_heads, group_size, HEAD_WIDTH).transpose(1, 2, 0, 3)
    grad_split = grad_cols.reshape(length, kv_heads, group_size, HEAD_WIDTH).transpose(1, 2, 0, 3)
    key_split = key_cols.reshape(length, kv_heads, HEAD_WIDTH).transpose(1, 0, 2)
    value_split = value_cols.reshape(length, kv_heads, HEAD_WIDTH).transpose(1, 0, 2)

    def per_group(inputs):
        return group_pass(inputs[0], inputs[1], inputs[2], inputs[3], allowed)

    query_parts, key_parts, value_parts = lax.map(
        per_group, (query_split, key_split, value_split, grad_split)
    )
    query_out = query_parts.transpose(2, 0, 1, 3).reshape(length, q_heads * HEAD_WIDTH)
    key_out = key_parts.transpose(1, 0, 2).reshape(length, kv_heads * HEAD_WIDTH)
    value_out = value_parts.transpose(1, 0, 2).reshape(length, kv_heads * HEAD_WIDTH)
    return (query_out, key_out, value_out)


def row_product(shard_rows, value_rows):
    return lax.dot_general(
        shard_rows, value_rows, (((0,), (0,)), ((), ())), preferred_element_type=jnp.float32
    )


def local(queries, key_states, section_value_states, out_grad, layer_input, doc_segments):
    query_head, key_head, value_head, grad_head = (
        lax.all_to_all(queries[0], "seq", split_axis=1, concat_axis=0, tiled=True),
        lax.all_to_all(key_states[0], "seq", split_axis=1, concat_axis=0, tiled=True),
        lax.all_to_all(section_value_states[0], "seq", split_axis=1, concat_axis=0, tiled=True),
        lax.all_to_all(out_grad[0], "seq", split_axis=1, concat_axis=0, tiled=True),
    )
    doc_ids = lax.all_gather(doc_segments[0], "seq", axis=0, tiled=True)
    query_out, key_out, value_out = attention_grads(
        query_head, key_head, value_head, grad_head, doc_ids
    )
    query_back, key_back = (
        lax.all_to_all(query_out, "seq", split_axis=0, concat_axis=1, tiled=True),
        lax.all_to_all(key_out, "seq", split_axis=0, concat_axis=1, tiled=True),
    )
    section_count = lax.axis_size("section")
    section_grad = row_product(lax.all_gather(layer_input[0], "seq", axis=0, tiled=True), value_out)
    width_rows = section_grad.shape[0]
    pieces = section_grad.reshape(section_count, width_rows // section_count, section_grad.shape[1])
    received = lax.all_to_all(pieces, "section", split_axis=0, concat_axis=0, tiled=True)
    summed = received + received[::-1]
    returned = lax.all_to_all(
        summed.astype(jnp.bfloat16), "section", split_axis=0, concat_axis=0, tiled=True
    ).astype(summed.dtype)
    paired = returned.reshape(section_grad.shape)
    return (query_back[None], key_back[None], paired.astype(jnp.bfloat16)[None])


def solution(mesh):
    in_specs = (
        P("section", "seq", None),
        P("section", "seq", None),
        P("section", "seq", None),
        P("section", "seq", None),
        P("section", "seq", None),
        P("section", "seq"),
    )
    out_specs = (P("section", "seq", None), P("section", "seq", None), P("section", None, "seq"))
    return jax.shard_map(local, mesh=mesh, in_specs=in_specs, out_specs=out_specs, check_vma=False)
```

profile of v0, /device:TPU:8, one launch (start us, length us, event | category | flops | bytes accessed | tf_op | source)
XLA Modules:
  0.0 556.8 jit_solution(17774618715415717449)
XLA Ops:
  9.0 3.7 all-to-all-start.2
  14.6 3.5 all-to-all-done.2
  27.3 4.2 all-to-all-start
  31.5 4.5 all_to_all.81
  36.0 4.1 copy.60
  40.1 14.6 %all-to-all-done = bf16[128,4,2048]{2,0,1:T(8,128)(2,1)S(1)} async-done(((bf16[128,4,2048]{2,0,1:T(8,128)(2,1)}), bf16[128,4,2048]{2,0,1:T(8,128)(2,1)S(1)}, u32[]{:S(2)}, u32[]{:S(2)}) %all-to-all-start) | async-done | bytes 2097184 | tf_op jit(solution)/shard_map/all_to_all | solution.py:78
  56.0 4.5 all-to-all-start.1
  61.3 35.5 %all-gather = s32[1,512]{1,0:T(1,128)S(1)} all-gather(s32[1,128]{1,0:T(1,128)S(1)} %copy-done.7), channel_id=2, replica_groups=mesh['section'=8,'seq'=4] {'seq'}, dimensions={1}, use_global_device_ids=true | all-gather | bytes 2560 | tf_op jit(solution)/shard_map/all_gather | solution.py:83
  99.3 3.5 copy.83
  102.8 111.3 %while.32 = (s32[]{:T(128)}, bf16[2,8,512,128]{3,2,1,0:T(8,128)(2,1)}, bf16[2,512,128]{2,1,0:T(8,128)(2,1)}, bf16[2,512,128]{1,2,0:T(8,128)(2,1)}, bf16[2,8,512,...) while((s32[]{:T(128)}, ...), condition=%wide.region_6.7_spmd.clone, body=%wide.region_0.6_spmd.clone.sunk | while | flops 407894528 | bytes 43799096 | solution.py:61
  106.5 48.0 %while.33 = (s32[]{:T(128)}, f32[512,128]{1,0:T(8,128)S(1)}, f32[512,128]{1,0:T(8,128)S(1)}, bf16[8,512,128]{2,1,0:T(8,128)(2,1)}, bf16[8,512,128]{2,1,0:T(8,128...) while((s32[]{:T(128)}, f32[512,128]{1,0:T(8,128)S(1)}, ...), condition=%wide.region_5.5_spmd.clone, body=%wide.region_1.4_spmd.clone.sunk | while | flops 406977024 | bytes 10242200 | solution.py:40
  162.3 47.9 %while.33 = (s32[]{:T(128)}, f32[512,128]{1,0:T(8,128)S(1)}, f32[512,128]{1,0:T(8,128)S(1)}, bf16[8,512,128]{2,1,0:T(8,128)(2,1)}, bf16[8,512,128]{2,1,0:T(8,128...) while((s32[]{:T(128)}, f32[512,128]{1,0:T(8,128)S(1)}, ...), condition=%wide.region_5.5_spmd.clone, body=%wide.region_1.4_spmd.clone.sunk | while | flops 406977024 | bytes 10242200 | solution.py:40
  216.2 4.2 all-to-all-start.5
  220.5 5.8 %fusion.25 = f32[256,8192]{1,0:T(8,128)S(1)} fusion(bf16[512,256]{0,1:T(8,128)(2,1)} %bitcast.137, bf16[1,512,8192]{2,1,0:T(8,128)(2,1)} %all-gather.4.cloned.1.call-done), kind=kOutput, calls=%fused_computation.45 | convolution fusion | flops 2147483648 | bytes 17039360 | tf_op jit(solution)/shard_map/dot_general | solution.py:71
  226.3 4.1 copy.89
  230.4 5.5 all-to-all-start.6
  241.1 175.2 %all-to-all-done.6 = f32[8,1024,256]{1,2,0:T(8,128)} async-done(((f32[8,1024,256]{1,2,0:T(8,128)}), f32[8,1024,256]{1,2,0:T(8,128)}, u32[]{:S(2)}, u32[]{:S(2)}) %all-to-all-start.6) | async-done | bytes 8388640 | tf_op jit(solution)/shard_map/all_to_all | solution.py:95
  416.2 4.2 all-to-all-start.4
  420.4 9.3 %fusion.24 = bf16[8,1024,256]{1,2,0:T(8,128)(2,1)} fusion(f32[8,1024,256]{1,2,0:T(8,128)} %all-to-all-done.6), kind=kLoop, calls=%fused_computation.43 | loop fusion | flops 4194304 | bytes 12582912 | tf_op jit(solution)/shard_map/convert_element_type | solution.py:98
  429.7 15.8 %all-to-all-done.4 = bf16[4,128,2048]{2,1,0:T(8,128)(2,1)S(1)} async-done(((bf16[4,128,2048]{2,1,0:T(8,128)(2,1)}), bf16[4,128,2048]{2,1,0:T(8,128)(2,1)S(1)}, u32[]{:S(2)}, u32[]{:S(2)}) %all-to-all-start.4) | async-done | bytes 2097184 | tf_op jit(solution)/shard_map/all_to_all | solution.py:88
  445.5 7.5 %all-to-all-start.7 = ((bf16[8,1024,256]{1,2,0:T(8,128)(2,1)}), bf16[8,1024,256]{1,2,0:T(8,128)(2,1)}, u32[]{:S(2)}, u32[]{:S(2)}) async-start(bf16[8,1024,256]{1,2,0:T(8,128)(2,1)} %fusion.24), calls=%async_computation.7 | async-start | bytes 8388608 | tf_op jit(solution)/shard_map/all_to_all | solution.py:97
  456.5 4.1 copy.74
  460.5 83.0 %all-to-all-done.7 = bf16[8,1024,256]{1,2,0:T(8,128)(2,1)} async-done(((bf16[8,1024,256]{1,2,0:T(8,128)(2,1)}), bf16[8,1024,256]{1,2,0:T(8,128)(2,1)}, u32[]{:S(2)}, u32[]{:S(2)}) %all-to-all-start.7) | async-done | bytes 4194336 | tf_op jit(solution)/shard_map/all_to_all | solution.py:97
  543.5 6.4 %copy.73 = bf16[8,1024,256]{2,1,0:T(8,128)(2,1)} copy(bf16[8,1024,256]{1,2,0:T(8,128)(2,1)} %all-to-all-done.7) | data formatting | bytes 8388608 | tf_op jit(solution)/shard_map/all_to_all | solution.py:97
  (226 shorter events, 138.6 us)
Async XLA Ops:
  9.0 9.1 %all-to-all-start.2 = ((bf16[128,4,256]{2,0,1:T(8,128)(2,1)}), bf16[128,4,256]{2,0,1:T(8,128)(2,1)S(1)}, u32[]{:S(2)}, u32[]{:S(2)}) async-start(bf16[128,4,256]{2,0,1:T(8,128)(2,1)} %copy.61), calls=%async_computation.2 | async-start | bytes 524288 | tf_op jit(solution)/shard_map/all_to_all | solution.py:79
  18.1 9.2 %all-to-all-start.3 = ((bf16[128,4,256]{2,0,1:T(8,128)(2,1)}), bf16[128,4,256]{2,0,1:T(8,128)(2,1)S(1)}, u32[]{:S(2)}, u32[]{:S(2)}) async-start(bf16[128,4,256]{2,0,1:T(8,128)(2,1)} %copy.62), calls=%async_computation.3 | async-start | bytes 524288 | tf_op jit(solution)/shard_map/all_to_all | solution.py:80
  27.3 27.3 %all-to-all-start = ((bf16[128,4,2048]{2,0,1:T(8,128)(2,1)}), bf16[128,4,2048]{2,0,1:T(8,128)(2,1)S(1)}, u32[]{:S(2)}, u32[]{:S(2)}) async-start(bf16[128,4,2048]{2,0,1:T(8,128)(2,1)} %copy.59), calls=%async_computation | async-start | bytes 4194304 | tf_op jit(solution)/shard_map/all_to_all | solution.py:78
  54.7 1.3 copy-start.2
  56.0 43.2 %all-to-all-start.1 = ((bf16[128,4,2048]{2,0,1:T(8,128)(2,1)}), bf16[128,4,2048]{2,0,1:T(8,128)(2,1)}, u32[]{:S(2)}, u32[]{:S(2)}) async-start(bf16[128,4,2048]{2,0,1:T(8,128)(2,1)} %copy.60), calls=%async_computation.1 | async-start | bytes 4194304 | tf_op jit(solution)/shard_map/all_to_all | solution.py:81
  60.5 0.8 copy-start.7
  60.5 159.9 %all-gather.4.cloned.1.call-start = ((), (), s32[]{:S(2)}) async-start(), calls=%async_computation.8 | async-start | bytes 10485760 | tf_op jit(solution)/shard_map/all_gather | solution.py:92
  102.8 2.2 copy-start
  102.8 2.3 copy-start.3
  154.5 3.2 copy-start.5
  154.5 4.0 copy-start.1
  154.5 4.0 copy-start.4
  157.8 0.7 copy-start.6
  158.5 2.2 copy-start
  158.5 2.3 copy-start.3
  210.1 3.2 copy-start.5
  210.1 4.0 copy-start.1
  210.1 4.0 copy-start.4
  213.4 0.7 copy-start.6
  216.2 14.1 %all-to-all-start.5 = ((bf16[4,128,256]{2,1,0:T(8,128)(2,1)}), bf16[4,128,256]{2,1,0:T(8,128)(2,1)S(1)}, u32[]{:S(2)}, u32[]{:S(2)}) async-start(bf16[4,128,256]{2,1,0:T(8,128)(2,1)} %all_to_all.93), calls=%async_computation.5 | async-start | bytes 524288 | tf_op jit(solution)/shard_map/all_to_all | solution.py:89
  230.4 185.9 %all-to-all-start.6 = ((f32[8,1024,256]{1,2,0:T(8,128)}), f32[8,1024,256]{1,2,0:T(8,128)}, u32[]{:S(2)}, u32[]{:S(2)}) async-start(f32[8,1024,256]{1,2,0:T(8,128)} %bitcast.122), calls=%async_computation.6 | async-start | bytes 16777216 | tf_op jit(solution)/shard_map/all_to_all | solution.py:95
  416.2 29.3 %all-to-all-start.4 = ((bf16[4,128,2048]{2,1,0:T(8,128)(2,1)}), bf16[4,128,2048]{2,1,0:T(8,128)(2,1)S(1)}, u32[]{:S(2)}, u32[]{:S(2)}) async-start(bf16[4,128,2048]{2,1,0:T(8,128)(2,1)} %all_to_all.90), calls=%async_computation.4 | async-start | bytes 4194304 | tf_op jit(solution)/shard_map/all_to_all | solution.py:88
  445.5 98.0 %all-to-all-start.7 = ((bf16[8,1024,256]{1,2,0:T(8,128)(2,1)}), bf16[8,1024,256]{1,2,0:T(8,128)(2,1)}, u32[]{:S(2)}, u32[]{:S(2)}) async-start(bf16[8,1024,256]{1,2,0:T(8,128)(2,1)} %fusion.24), calls=%async_computation.7 | async-start | bytes 8388608 | tf_op jit(solution)/shard_map/all_to_all | solution.py:97
Sparse Core Ops, SparseCore 0:
  63.2 97.2 all-gather.3
where the time goes:
time: 564 us; the launch traced here: 557 us
  waiting for transfers between devices  293 us (52%)
  matrix products  77.9 us (14%)
  local copies, waits for them, and re-layouts  64.2 us (11%)
  starting transfers between devices  37.2 us (7%)
  blocking collectives  35.5 us (6%)
  other arithmetic  34.1 us (6%)
  between operations  14.2 us (3%)
    all_to_all x1, waiting for transfers between devices, local(): lax.all_to_all(pieces, 'section', split_axis=0, concat_axis=0, tiled=True)  175 us
    all_to_all x1, waiting for transfers between devices, local(): lax.all_to_all(summed.astype(jnp.bfloat16), 'section', split_axis=0, conc...  83 us
    all_gather x1, blocking collectives, local(): doc_ids = lax.all_gather(doc_segments[0], 'seq', axis=0, tiled=True)  35.5 us
    dot_general x16, matrix products, one_head(): dprobs = jnp.dot(grad_one, value_col.T, preferred_element_type=jnp.float32)  20.3 us
    dot_general x16, matrix products, one_head(): jnp.dot(probs_low.T, grad_one, preferred_element_type=jnp.float32)  19.5 us
    reduce_sum x16, other arithmetic, one_head(): jnp.sum(grad_one.astype(jnp.float32) * attended.astype(jnp.float32), axis...  17.1 us
    dot_general x16, matrix products, one_head(): jnp.dot(dscores, key_col, preferred_element_type=jnp.float32)  16 us
    all_to_all x1, waiting for transfers between devices, local(): lax.all_to_all(query_out, 'seq', split_axis=0, concat_axis=1, tiled=True)  15.8 us
  transfers between devices with their start and end apart: 9, of which 5 were waited for; matrix products, arithmetic and copies ran while one was open for 27% of the time, Pallas kernels for 0%

commit v1 on v0

--- a/solution.py
+++ b/solution.py
@@ -74,6 +74,9 @@
 
 
 def local(queries, key_states, section_value_states, out_grad, layer_input, doc_segments):
+    section_count = lax.axis_size("section")
+    mirror = [(i, section_count - 1 - i) for i in range(section_count)]
+    mirror_rows = lax.ppermute(layer_input[0], "section", mirror)
     query_head, key_head, value_head, grad_head = (
         lax.all_to_all(queries[0], "seq", split_axis=1, concat_axis=0, tiled=True),
         lax.all_to_all(key_states[0], "seq", split_axis=1, concat_axis=0, tiled=True),
@@ -88,16 +91,16 @@
         lax.all_to_all(query_out, "seq", split_axis=0, concat_axis=1, tiled=True),
         lax.all_to_all(key_out, "seq", split_axis=0, concat_axis=1, tiled=True),
     )
-    section_count = lax.axis_size("section")
-    section_grad = row_product(lax.all_gather(layer_input[0], "seq", axis=0, tiled=True), value_out)
-    width_rows = section_grad.shape[0]
-    pieces = section_grad.reshape(section_count, width_rows // section_count, section_grad.shape[1])
-    received = lax.all_to_all(pieces, "section", split_axis=0, concat_axis=0, tiled=True)
-    summed = received + received[::-1]
-    returned = lax.all_to_all(
-        summed.astype(jnp.bfloat16), "section", split_axis=0, concat_axis=0, tiled=True
-    ).astype(summed.dtype)
-    paired = returned.reshape(section_grad.shape)
+    both_rows = jnp.concatenate([layer_input[0], mirror_rows], axis=0)
+    gathered = lax.all_gather(both_rows, "seq", axis=0, tiled=True)
+    mirror_value = lax.ppermute(value_out, "section", mirror)
+    seq_count = lax.axis_size("seq")
+    chunk = value_out.shape[0] // seq_count
+    both_values = jnp.stack(
+        [value_out.reshape(seq_count, chunk, -1), mirror_value.reshape(seq_count, chunk, -1)],
+        axis=1,
+    ).reshape(2 * value_out.shape[0], value_out.shape[1])
+    paired = row_product(gathered, both_values)
     return (query_back[None], key_back[None], paired.astype(jnp.bfloat16)[None])
 
 

time: 564 us -> 335 us (0.59)
  waiting for transfers between devices: 293 us -> 100 us
  starting transfers between devices: 37.2 us -> 23.8 us
  local copies, waits for them, and re-layouts: 64.2 us -> 53.2 us
  blocking collectives: 35.5 us -> 26 us
  matrix products: 77.9 us -> 85 us
    all_to_all x2 -> x0, waiting for transfers between devices: 258 us -> none  [the longest x1 175 us: local(): lax.all_to_all(pieces, 'section', split_axis=0, concat_axis=0, tiled=True)]
    ppermute x0 -> x2, waiting for transfers between devices: none -> 39.8 us  [the longest x1 33.2 us: local(): mirror_rows = lax.ppermute(layer_input[0], 'section', mirror)]
    all_to_all x1, waiting for transfers between devices: 15.8 us -> 38.7 us  [local(): lax.all_to_all(query_out, 'seq', split_axis=0, concat_axis=1, tiled=True)]
    all_to_all x2 -> x0, starting transfers between devices: 12.9 us -> none  [the longest x1 7.47 us: local(): lax.all_to_all(summed.astype(jnp.bfloat16), 'section', split_axis=0, conc...]
    all_gather x1, blocking collectives: 35.5 us -> 26 us  [local(): doc_ids = lax.all_gather(doc_segments[0], 'seq', axis=0, tiled=True)]
    convert_element_type x1 -> x0, other arithmetic: 9.3 us -> none  [local(): summed.astype(jnp.bfloat16)]
    dot_general x1, matrix products: 5.82 us -> 12.6 us  [row_product(): lax.dot_general(shard_rows, value_rows, (((0,), (0,)), ((), ())), preferr...]
    all_to_all x1 -> x0, local copies, waits for them, and re-layouts: 6.42 us -> none  [local(): lax.all_to_all(summed.astype(jnp.bfloat16), 'section', split_axis=0, conc...]
  transfers between devices with their start and end apart: 9 -> 9, of which waited for: 5 -> 6; matrix products, arithmetic and copies ran while one was open for 27% -> 40% of each run, Pallas kernels for 0% -> 0%
where the time goes in v1:
time: 335 us; the launch traced here: 333 us
  waiting for transfers between devices  100 us (30%)
  matrix products  85 us (25%)
  local copies, waits for them, and re-layouts  53.2 us (16%)
  other arithmetic  29 us (9%)
  blocking collectives  26 us (8%)
  starting transfers between devices  23.8 us (7%)
  between operations  14.2 us (4%)
    all_to_all x1, waiting for transfers between devices, local(): lax.all_to_all(query_out, 'seq', split_axis=0, concat_axis=1, tiled=True)  38.7 us
    ppermute x1, waiting for transfers between devices, local(): mirror_rows = lax.ppermute(layer_input[0], 'section', mirror)  33.2 us
    all_gather x1, blocking collectives, local(): doc_ids = lax.all_gather(doc_segments[0], 'seq', axis=0, tiled=True)  26 us
    dot_general x16, matrix products, one_head(): dprobs = jnp.dot(grad_one, value_col.T, preferred_element_type=jnp.float32)  20.4 us
    dot_general x16, matrix products, one_head(): jnp.dot(probs_low.T, grad_one, preferred_element_type=jnp.float32)  19.7 us
    reduce_sum x16, other arithmetic, one_head(): jnp.sum(grad_one.astype(jnp.float32) * attended.astype(jnp.float32), axis...  17.2 us
    dot_general x16, matrix products, one_head(): jnp.dot(dscores, key_col, preferred_element_type=jnp.float32)  16.1 us
    all_to_all x1, waiting for transfers between devices, local(): lax.all_to_all(queries[0], 'seq', split_axis=1, concat_axis=0, tiled=True)  14.6 us
  transfers between devices with their start and end apart: 9, of which 6 were waited for; matrix products, arithmetic and copies ran while one was open for 40% of the time, Pallas kernels for 0%

profile of v1, /device:TPU:8, one launch (start us, length us, event | category | flops | bytes accessed | tf_op | source)
XLA Modules:
  0.0 332.5 jit_solution(17759359656926367715)
XLA Ops:
  9.0 3.7 %all-to-all-start.2 = ((bf16[128,4,256]{2,0,1:T(8,128)(2,1)}), bf16[128,4,256]{2,0,1:T(8,128)(2,1)S(1)}, u32[]{:S(2)}, u32[]{:S(2)}) async-start(bf16[128,4,256]{2,0,1:T(8,128)(2,1)} %copy.27), calls=%async_computation.2 | async-start | bytes 524288 | tf_op jit(solution)/shard_map/all_to_all | solution.py:82
  14.6 3.5 %all-to-all-done.2 = bf16[128,4,256]{2,0,1:T(8,128)(2,1)S(1)} async-done(((bf16[128,4,256]{2,0,1:T(8,128)(2,1)}), bf16[128,4,256]{2,0,1:T(8,128)(2,1)S(1)}, u32[]{:S(2)}, u32[]{:S(2)}) %all-to-all-start.2) | async-done | bytes 262176 | tf_op jit(solution)/shard_map/all_to_all | solution.py:82
  18.1 3.4 %all-to-all-start.3 = ((bf16[128,4,256]{2,0,1:T(8,128)(2,1)}), bf16[128,4,256]{2,0,1:T(8,128)(2,1)S(1)}, u32[]{:S(2)}, u32[]{:S(2)}) async-start(bf16[128,4,256]{2,0,1:T(8,128)(2,1)} %copy.28), calls=%async_computation.3 | async-start | bytes 524288 | tf_op jit(solution)/shard_map/all_to_all | solution.py:83
  21.5 3.3 all_to_all.72
  27.3 4.2 %all-to-all-start = ((bf16[128,4,2048]{2,0,1:T(8,128)(2,1)}), bf16[128,4,2048]{2,0,1:T(8,128)(2,1)S(1)}, u32[]{:S(2)}, u32[]{:S(2)}) async-start(bf16[128,4,2048]{2,0,1:T(8,128)(2,1)} %copy.25), calls=%async_computation | async-start | bytes 4194304 | tf_op jit(solution)/shard_map/all_to_all | solution.py:81
  31.5 4.5 %all_to_all.75 = bf16[128,4,2048]{2,1,0:T(4,128)(2,1)} reshape(bf16[1,128,8192]{2,1,0:T(8,128)(2,1)} %param.13) | data formatting | bytes 4194304 | tf_op jit(solution)/shard_map/all_to_all | solution.py:84
  36.0 4.1 %copy.26 = bf16[128,4,2048]{2,0,1:T(8,128)(2,1)} copy(bf16[128,4,2048]{2,1,0:T(4,128)(2,1)} %all_to_all.75) | data formatting | bytes 4194304 | tf_op jit(solution)/shard_map/all_to_all | solution.py:84
  40.1 14.6 %all-to-all-done = bf16[128,4,2048]{2,0,1:T(8,128)(2,1)S(1)} async-done(((bf16[128,4,2048]{2,0,1:T(8,128)(2,1)}), bf16[128,4,2048]{2,0,1:T(8,128)(2,1)S(1)}, u32[]{:S(2)}, u32[]{:S(2)}) %all-to-all-start) | async-done | bytes 2097184 | tf_op jit(solution)/shard_map/all_to_all | solution.py:81
  54.7 4.4 %all-to-all-start.1 = ((bf16[128,4,2048]{2,0,1:T(8,128)(2,1)}), bf16[128,4,2048]{2,0,1:T(8,128)(2,1)}, u32[]{:S(2)}, u32[]{:S(2)}) async-start(bf16[128,4,2048]{2,0,1:T(8,128)(2,1)} %copy.26), calls=%async_computation.1 | async-start | bytes 4194304 | tf_op jit(solution)/shard_map/all_to_all | solution.py:84
  59.2 26.0 %all-gather = s32[1,512]{1,0:T(1,128)S(1)} all-gather(s32[1,128]{1,0:T(1,128)S(1)} %copy-done.8), channel_id=2, replica_groups=mesh['section'=8,'seq'=4] {'seq'}, dimensions={1}, use_global_device_ids=true | all-gather | bytes 2560 | tf_op jit(solution)/shard_map/all_gather | solution.py:86
  87.7 3.7 %copy.48 = bf16[64,8,16,128]{3,2,1,0:T(8,128)(2,1)} copy(bf16[64,8,16,128]{3,1,2,0:T(8,128)(2,1)} %bitcast.38) | data formatting | bytes 4194304
  91.4 33.2 %collective-permute-done = bf16[128,8192]{1,0:T(8,128)(2,1)} collective-permute-done((bf16[128,8192]{1,0:T(8,128)(2,1)}, bf16[128,8192]{1,0:T(8,128)(2,1)}, u32[]{:S(2)}, u32[]{:S(2)}) %collective-permute-start) | collective-permute-done | bytes 2097184 | tf_op jit(solution)/shard_map/ppermute | solution.py:79
  124.6 4.0 %pad_maximum_fusion = bf16[256,8192]{1,0:T(8,128)(2,1)} fusion(bf16[128,8192]{1,0:T(8,128)(2,1)} %collective-permute-done, bf16[128,8192]{1,0:T(8,128)(2,1)S(1)} %bitcast.127), kind=kLoop, calls=%fused_computation.43 | loop fusion | flops 8388608 | bytes 8388608 | tf_op jit(solution)/shard_map/concatenate | solution.py:94
  128.6 110.8 %while.32 = (s32[]{:T(128)}, bf16[2,8,512,128]{3,2,1,0:T(8,128)(2,1)}, bf16[2,512,128]{2,1,0:T(8,128)(2,1)}, bf16[2,512,128]{2,1,0:T(8,128)(2,1)}, bf16[2,8,512,...) while((s32[]{:T(128)}, ...), condition=%wide.region_6.7_spmd.clone, body=%wide.region_0.6_spmd.clone.sunk | while | flops 407894528 | bytes 49566240 | solution.py:61
  132.8 48.1 %while.33 = (s32[]{:T(128)}, f32[512,128]{1,0:T(8,128)S(1)}, f32[512,128]{1,0:T(8,128)S(1)}, bf16[8,512,128]{2,1,0:T(8,128)(2,1)}, bf16[8,512,128]{2,1,0:T(8,128...) while((s32[]{:T(128)}, f32[512,128]{1,0:T(8,128)S(1)}, ...), condition=%wide.region_5.5_spmd.clone, body=%wide.region_1.4_spmd.clone.sunk | while | flops 406977024 | bytes 10242200 | solution.py:40
  188.2 48.1 %while.33 = (s32[]{:T(128)}, f32[512,128]{1,0:T(8,128)S(1)}, f32[512,128]{1,0:T(8,128)S(1)}, bf16[8,512,128]{2,1,0:T(8,128)(2,1)}, bf16[8,512,128]{2,1,0:T(8,128...) while((s32[]{:T(128)}, f32[512,128]{1,0:T(8,128)S(1)}, ...), condition=%wide.region_5.5_spmd.clone, body=%wide.region_1.4_spmd.clone.sunk | while | flops 406977024 | bytes 10242200 | solution.py:40
  241.5 4.2 %all-to-all-start.5 = ((bf16[4,128,256]{2,1,0:T(8,128)(2,1)}), bf16[4,128,256]{2,1,0:T(8,128)(2,1)S(1)}, u32[]{:S(2)}, u32[]{:S(2)}) async-start(bf16[4,128,256]{2,1,0:T(8,128)(2,1)} %all_to_all.87), calls=%async_computation.5 | async-start | bytes 524288 | tf_op jit(solution)/shard_map/all_to_all | solution.py:92
  245.8 2.9 copy.33
  251.0 3.8 %all-to-all-done.5 = bf16[4,128,256]{2,1,0:T(8,128)(2,1)S(1)} async-done(((bf16[4,128,256]{2,1,0:T(8,128)(2,1)}), bf16[4,128,256]{2,1,0:T(8,128)(2,1)S(1)}, u32[]{:S(2)}, u32[]{:S(2)}) %all-to-all-start.5) | async-done | bytes 262176 | tf_op jit(solution)/shard_map/all_to_all | solution.py:92
  254.8 3.8 %all-to-all-start.4 = ((bf16[4,128,2048]{2,1,0:T(8,128)(2,1)}), bf16[4,128,2048]{2,1,0:T(8,128)(2,1)S(1)}, u32[]{:S(2)}, u32[]{:S(2)}) async-start(bf16[4,128,2048]{2,1,0:T(8,128)(2,1)} %all_to_all.84), calls=%async_computation.4 | async-start | bytes 4194304 | tf_op jit(solution)/shard_map/all_to_all | solution.py:91
  260.9 6.7 %collective-permute-done.1 = bf16[512,256]{0,1:T(8,128)(2,1)S(1)} collective-permute-done((bf16[512,256]{0,1:T(8,128)(2,1)}, bf16[512,256]{0,1:T(8,128)(2,1)S(1)}, u32[]{:S(2)}, u32[]{:S(2)}) %collective-permute-start.1) | collective-permute-done | bytes 262176 | tf_op jit(solution)/shard_map/ppermute | solution.py:96
  267.9 38.7 %all-to-all-done.4 = bf16[4,128,2048]{2,1,0:T(8,128)(2,1)S(1)} async-done(((bf16[4,128,2048]{2,1,0:T(8,128)(2,1)}), bf16[4,128,2048]{2,1,0:T(8,128)(2,1)S(1)}, u32[]{:S(2)}, u32[]{:S(2)}) %all-to-all-start.4) | async-done | bytes 2097184 | tf_op jit(solution)/shard_map/all_to_all | solution.py:91
  309.0 4.1 %copy.41 = bf16[1,128,8192]{2,1,0:T(8,128)(2,1)} copy(bf16[1,128,8192]{1,2,0:T(8,128)(2,1)} %bitcast.124) | data formatting | bytes 4194304
  313.1 12.6 %fusion.24 = bf16[1,8192,256]{2,1,0:T(8,128)(2,1)} fusion(bf16[1024,8192]{1,0:T(8,128)(2,1)} %all-gather.3.cloned.1.call-done, bf16[1024,256]{1,0:T(8,128)(2,1)S(1)} %bitcast.136), kind=kOutput, calls=%fused_computation.42 | convolution fusion | flops 4297064448 | bytes 21495808 | tf_op jit(solution)/shard_map/dot_general | solution.py:71
  (228 shorter events, 128.0 us)
Async XLA Ops:
  9.0 9.1 %all-to-all-start.2 = ((bf16[128,4,256]{2,0,1:T(8,128)(2,1)}), bf16[128,4,256]{2,0,1:T(8,128)(2,1)S(1)}, u32[]{:S(2)}, u32[]{:S(2)}) async-start(bf16[128,4,256]{2,0,1:T(8,128)(2,1)} %copy.27), calls=%async_computation.2 | async-start | bytes 524288 | tf_op jit(solution)/shard_map/all_to_all | solution.py:82
  18.1 9.2 %all-to-all-start.3 = ((bf16[128,4,256]{2,0,1:T(8,128)(2,1)}), bf16[128,4,256]{2,0,1:T(8,128)(2,1)S(1)}, u32[]{:S(2)}, u32[]{:S(2)}) async-start(bf16[128,4,256]{2,0,1:T(8,128)(2,1)} %copy.28), calls=%async_computation.3 | async-start | bytes 524288 | tf_op jit(solution)/shard_map/all_to_all | solution.py:83
  27.3 27.3 %all-to-all-start = ((bf16[128,4,2048]{2,0,1:T(8,128)(2,1)}), bf16[128,4,2048]{2,0,1:T(8,128)(2,1)S(1)}, u32[]{:S(2)}, u32[]{:S(2)}) async-start(bf16[128,4,2048]{2,0,1:T(8,128)(2,1)} %copy.25), calls=%async_computation | async-start | bytes 4194304 | tf_op jit(solution)/shard_map/all_to_all | solution.py:81
  31.5 93.1 %collective-permute-start = (bf16[128,8192]{1,0:T(8,128)(2,1)}, bf16[128,8192]{1,0:T(8,128)(2,1)}, u32[]{:S(2)}, u32[]{:S(2)}) collective-permute-start(bf16[128,8192]{1,0:T(8,128)(2,1)} %bitcast.126), channel_id=1, source_target_pairs={{0,28},{4,24},{8,20},{12,16},{16,12},{20,8},{24,4},{28,0},{1,29},{... | collective-permute-start | bytes 6291464 | tf_op jit(solution)/shard_map/ppermute | solution.py:79
  40.1 19.1 %copy-start.8 = (s32[1,128]{1,0:T(1,128)S(1)}, s32[1,128]{1,0:T(1,128)}, u32[]{:S(2)}) copy-start(s32[1,128]{1,0:T(1,128)} %param.15) | copy-start | bytes 1540
  54.7 4.5 %copy-start.3 = (bf16[128,4,2048]{2,0,1:T(8,128)(2,1)}, bf16[128,4,2048]{2,0,1:T(8,128)(2,1)S(1)}, u32[]{:S(2)}) copy-start(bf16[128,4,2048]{2,0,1:T(8,128)(2,1)S(1)} %all-to-all-done) | copy-start | bytes 6291460
  54.7 33.0 %all-to-all-start.1 = ((bf16[128,4,2048]{2,0,1:T(8,128)(2,1)}), bf16[128,4,2048]{2,0,1:T(8,128)(2,1)}, u32[]{:S(2)}, u32[]{:S(2)}) async-start(bf16[128,4,2048]{2,0,1:T(8,128)(2,1)} %copy.26), calls=%async_computation.1 | async-start | bytes 4194304 | tf_op jit(solution)/shard_map/all_to_all | solution.py:84
  59.1 253.9 %all-gather.3.cloned.1.call-start = ((), (), s32[]{:S(2)}) async-start(), calls=%async_computation.6 | async-start | bytes 20971520 | tf_op jit(solution)/shard_map/all_gather | solution.py:95
  87.7 36.9 %copy-start.6 = (bf16[1,128,8192]{2,1,0:T(8,128)(2,1)S(1)}, bf16[1,128,8192]{2,1,0:T(8,128)(2,1)}, u32[]{:S(2)}) copy-start(bf16[1,128,8192]{2,1,0:T(8,128)(2,1)} %param.14) | copy-start | bytes 6291460
  128.6 1.3 copy-start
  128.7 4.1 %copy-start.4 = (bf16[2,512,128]{2,1,0:T(8,128)(2,1)}, bf16[2,512,128]{2,1,0:T(8,128)(2,1)S(1)}, u32[]{:S(2)}) copy-start(bf16[2,512,128]{2,1,0:T(8,128)(2,1)S(1)} %get-tuple-element.437) | copy-start | bytes 786436 | tf_op jit(solution)/shard_map/while
  129.9 1.6 copy-start.2
  180.9 3.2 copy-start.1
  180.9 3.2 copy-start.5
  184.1 1.3 copy-start
  184.1 4.1 %copy-start.4 = (bf16[2,512,128]{2,1,0:T(8,128)(2,1)}, bf16[2,512,128]{2,1,0:T(8,128)(2,1)S(1)}, u32[]{:S(2)}) copy-start(bf16[2,512,128]{2,1,0:T(8,128)(2,1)S(1)} %get-tuple-element.437) | copy-start | bytes 786436 | tf_op jit(solution)/shard_map/while
  185.4 1.6 copy-start.2
  236.3 3.2 copy-start.1
  236.3 3.2 copy-start.5
  241.5 13.3 %all-to-all-start.5 = ((bf16[4,128,256]{2,1,0:T(8,128)(2,1)}), bf16[4,128,256]{2,1,0:T(8,128)(2,1)S(1)}, u32[]{:S(2)}, u32[]{:S(2)}) async-start(bf16[4,128,256]{2,1,0:T(8,128)(2,1)} %all_to_all.87), calls=%async_computation.5 | async-start | bytes 524288 | tf_op jit(solution)/shard_map/all_to_all | solution.py:92
  251.0 7.6 %copy-start.7 = (bf16[2,512,128]{2,1,0:T(8,128)(2,1)S(1)}, bf16[2,512,128]{2,1,0:T(8,128)(2,1)}, u32[]{:S(2)}) copy-start(bf16[2,512,128]{2,1,0:T(8,128)(2,1)} %get-tuple-element.103) | copy-start | bytes 786436
  254.8 51.7 %all-to-all-start.4 = ((bf16[4,128,2048]{2,1,0:T(8,128)(2,1)}), bf16[4,128,2048]{2,1,0:T(8,128)(2,1)S(1)}, u32[]{:S(2)}, u32[]{:S(2)}) async-start(bf16[4,128,2048]{2,1,0:T(8,128)(2,1)} %all_to_all.84), calls=%async_computation.4 | async-start | bytes 4194304 | tf_op jit(solution)/shard_map/all_to_all | solution.py:91
  259.4 8.2 %collective-permute-start.1 = (bf16[512,256]{0,1:T(8,128)(2,1)}, bf16[512,256]{0,1:T(8,128)(2,1)S(1)}, u32[]{:S(2)}, u32[]{:S(2)}) collective-permute-start(bf16[512,256]{0,1:T(8,128)(2,1)} %bitcast.18), channel_id=1, source_target_pairs={{0,28},{4,24},{8,20},{12,16},{16,12},{20,8},{24,4},{28,0},{1,29},{... | collective-permute-start | bytes 786440 | tf_op jit(solution)/shard_map/ppermute | solution.py:96
Sparse Core Ops, SparseCore 0:
  128.7 182.3 all-gather.2

commit v2 on v1

v2 whole, which is shorter than its diff:
```python
import math

import jax
import jax.numpy as jnp
from jax import lax
from jax.experimental import pallas as pl
from jax.experimental.pallas import tpu as pltpu
from jax.sharding import PartitionSpec as P

HEAD_WIDTH = 128


def attention_kernel(query_ref, key_ref, value_ref, grad_ref, doc_col_ref, doc_row_ref,
                     query_out_ref, key_out_ref, value_out_ref):
    head, tile = pl.program_id(1), pl.program_id(2)
    rows, length = query_ref.shape[0], key_ref.shape[0]
    scale_factor = 1.0 / math.sqrt(key_ref.shape[1])

    @pl.when((head == 0) & (tile == 0))
    def _():
        key_out_ref[...] = jnp.zeros(key_out_ref.shape, jnp.float32)
        value_out_ref[...] = jnp.zeros(value_out_ref.shape, jnp.float32)

    query_one, grad_one = query_ref[...], grad_ref[...]
    key_col, value_col = key_ref[...], value_ref[...]
    row_pos = tile * rows + lax.broadcasted_iota(jnp.int32, (rows, length), 0)
    col_pos = lax.broadcasted_iota(jnp.int32, (rows, length), 1)
    allowed = (row_pos >= col_pos) & (doc_col_ref[...] == doc_row_ref[...])
    contract_last = (((1,), (1,)), ((), ()))
    contract_first = (((0,), (0,)), ((), ()))
    scores = lax.dot_general(query_one, key_col, contract_last,
                             preferred_element_type=jnp.float32) * scale_factor
    scores = jnp.where(allowed, scores, -jnp.inf)
    row_max = jnp.max(scores, axis=1, keepdims=True)
    weights = jnp.exp(scores - row_max)
    attention = weights / jnp.sum(weights, axis=1, keepdims=True)
    probs_low = attention.astype(jnp.bfloat16)
    attended = jnp.dot(probs_low, value_col, preferred_element_type=jnp.float32).astype(jnp.bfloat16)
    row_delta = jnp.sum(grad_one.astype(jnp.float32) * attended.astype(jnp.float32),
                        axis=1, keepdims=True)
    dprobs = lax.dot_general(grad_one, value_col, contract_last,
                             preferred_element_type=jnp.float32)
    dscores = (attention * (dprobs - row_delta) * scale_factor).astype(jnp.bfloat16)
    query_out_ref[...] = jnp.dot(dscores, key_col,
                                 preferred_element_type=jnp.float32).astype(jnp.bfloat16)
    key_out_ref[...] += lax.dot_general(dscores, query_one, contract_first,
                                        preferred_element_type=jnp.float32)
    value_out_ref[...] += lax.dot_general(probs_low, grad_one, contract_first,
                                          preferred_element_type=jnp.float32)


def attention_grads(query_cols, key_cols, value_cols, grad_cols, doc_ids):
    length = query_cols.shape[0]
    kv_heads = key_cols.shape[1] // HEAD_WIDTH
    q_heads = query_cols.shape[1] // HEAD_WIDTH
    group_size = q_heads // kv_heads
    rows = min(length, 256)
    tiles = length // rows
    head_block = lambda g, h, t: (t, g * group_size + h)
    kv_block = lambda g, h, t: (0, g)
    query_out, key_acc, value_acc = pl.pallas_call(
        attention_kernel,
        grid=(kv_heads, group_size, tiles),
        in_specs=[
            pl.BlockSpec((rows, HEAD_WIDTH), head_block),
            pl.BlockSpec((length, HEAD_WIDTH), kv_block),
            pl.BlockSpec((length, HEAD_WIDTH), kv_block),
            pl.BlockSpec((rows, HEAD_WIDTH), head_block),
            pl.BlockSpec((rows, 1), lambda g, h, t: (t, 0)),
            pl.BlockSpec((1, length), lambda g, h, t: (0, 0)),
        ],
        out_specs=[
            pl.BlockSpec((rows, HEAD_WIDTH), head_block),
            pl.BlockSpec((length, HEAD_WIDTH), kv_block),
            pl.BlockSpec((length, HEAD_WIDTH), kv_block),
        ],
        out_shape=[
            jax.ShapeDtypeStruct(query_cols.shape, jnp.bfloat16),
            jax.ShapeDtypeStruct(key_cols.shape, jnp.float32),
            jax.ShapeDtypeStruct(value_cols.shape, jnp.float32),
        ],
        compiler_params=pltpu.CompilerParams(
            dimension_semantics=("arbitrary", "arbitrary", "arbitrary"),
            vmem_limit_bytes=48 * 1024 * 1024,
        ),
    )(query_cols, key_cols, value_cols, grad_cols, doc_ids.reshape(length, 1),
      doc_ids.reshape(1, length))
    return (query_out, key_acc.astype(jnp.bfloat16), value_acc.astype(jnp.bfloat16))


def row_product(shard_rows, value_rows):
    return lax.dot_general(
        shard_rows, value_rows, (((0,), (0,)), ((), ())), preferred_element_type=jnp.float32
    )


def local(queries, key_states, section_value_states, out_grad, layer_input, doc_segments):
    section_count = lax.axis_size("section")
    mirror = [(i, section_count - 1 - i) for i in range(section_count)]
    mirror_rows = lax.ppermute(layer_input[0], "section", mirror)
    query_head, key_head, value_head, grad_head = (
        lax.all_to_all(queries[0], "seq", split_axis=1, concat_axis=0, tiled=True),
        lax.all_to_all(key_states[0], "seq", split_axis=1, concat_axis=0, tiled=True),
        lax.all_to_all(section_value_states[0], "seq", split_axis=1, concat_axis=0, tiled=True),
        lax.all_to_all(out_grad[0], "seq", split_axis=1, concat_axis=0, tiled=True),
    )
    doc_ids = lax.all_gather(doc_segments[0], "seq", axis=0, tiled=True)
    query_out, key_out, value_out = attention_grads(
        query_head, key_head, value_head, grad_head, doc_ids
    )
    query_back, key_back = (
        lax.all_to_all(query_out, "seq", split_axis=0, concat_axis=1, tiled=True),
        lax.all_to_all(key_out, "seq", split_axis=0, concat_axis=1, tiled=True),
    )
    both_rows = jnp.concatenate([layer_input[0], mirror_rows], axis=0)
    gathered = lax.all_gather(both_rows, "seq", axis=0, tiled=True)
    mirror_value = lax.ppermute(value_out, "section", mirror)
    seq_count = lax.axis_size("seq")
    chunk = value_out.shape[0] // seq_count
    both_values = jnp.stack(
        [value_out.reshape(seq_count, chunk, -1), mirror_value.reshape(seq_count, chunk, -1)],
        axis=1,
    ).reshape(2 * value_out.shape[0], value_out.shape[1])
    paired = row_product(gathered, both_values)
    return (query_back[None], key_back[None], paired.astype(jnp.bfloat16)[None])


def solution(mesh):
    in_specs = (
        P("section", "seq", None),
        P("section", "seq", None),
        P("section", "seq", None),
        P("section", "seq", None),
        P("section", "seq", None),
        P("section", "seq"),
    )
    out_specs = (P("section", "seq", None), P("section", "seq", None), P("section", None, "seq"))
    return jax.shard_map(local, mesh=mesh, in_specs=in_specs, out_specs=out_specs, check_vma=False)
```

time: 335 us -> 348 us (1.039)
  waiting for transfers between devices: 100 us -> 189 us
  matrix products: 85 us -> 12.6 us
  Pallas kernels: 0 us -> 36.9 us
  local copies, waits for them, and re-layouts: 53.2 us -> 27.3 us
  other arithmetic: 29 us -> 4.15 us
  blocking collectives: 26 us -> 42.9 us
  starting transfers between devices: 23.8 us -> 20.2 us
    dot_general x96 -> x0, matrix products: 72.4 us -> none  [the longest x16 20.4 us: one_head(): dprobs = jnp.dot(grad_one, value_col.T, preferred_element_type=jnp.float32)]
    ppermute x1, waiting for transfers between devices: 33.2 us -> 91.9 us  [local(): mirror_rows = lax.ppermute(layer_input[0], 'section', mirror)]
    pallas_call x0 -> x1, Pallas kernels: none -> 36.9 us  [attention_grads(): pl.pallas_call(attention_kernel, grid=(kv_heads, group_size, tiles), in_s...]
    all_to_all x1, waiting for transfers between devices: 14.6 us -> 39.2 us  [local(): lax.all_to_all(queries[0], 'seq', split_axis=1, concat_axis=0, tiled=True)]
    reduce_sum x32 -> x0, other arithmetic: 20.3 us -> none  [the longest x16 17.2 us: one_head(): jnp.sum(grad_one.astype(jnp.float32) * attended.astype(jnp.float32), axis...]
    all_to_all x0 -> x1, blocking collectives: none -> 10.6 us  [local(): lax.all_to_all(key_out, 'seq', split_axis=0, concat_axis=1, tiled=True)]
    unnamed x14 -> x8, local copies, waits for them, and re-layouts: 10.9 us -> 2.24 us
    all_gather x1, blocking collectives: 26 us -> 32.3 us  [local(): doc_ids = lax.all_gather(doc_segments[0], 'seq', axis=0, tiled=True)]
  transfers between devices with their start and end apart: 9 -> 8, of which waited for: 6 -> 7; matrix products, arithmetic and copies ran while one was open for 40% -> 5% of each run, Pallas kernels for 0% -> 11%
where the time goes in v2:
time: 348 us; the launch traced here: 347 us
  waiting for transfers between devices  189 us (54%)
  blocking collectives  42.9 us (12%)
  Pallas kernels  36.9 us (11%)
  local copies, waits for them, and re-layouts  27.3 us (8%)
  starting transfers between devices  20.2 us (6%)
  between operations  14.2 us (4%)
  matrix products  12.6 us (4%)
  other arithmetic  4.15 us (1%)
    ppermute x1, waiting for transfers between devices, local(): mirror_rows = lax.ppermute(layer_input[0], 'section', mirror)  91.9 us
    all_to_all x1, waiting for transfers between devices, local(): lax.all_to_all(queries[0], 'seq', split_axis=1, concat_axis=0, tiled=True)  39.2 us
    all_to_all x1, waiting for transfers between devices, local(): lax.all_to_all(query_out, 'seq', split_axis=0, concat_axis=1, tiled=True)  38.5 us
    pallas_call x1, Pallas kernels, attention_grads(): pl.pallas_call(attention_kernel, grid=(kv_heads, group_size, tiles), in_s...  36.9 us
    all_gather x1, blocking collectives, local(): doc_ids = lax.all_gather(doc_segments[0], 'seq', axis=0, tiled=True)  32.3 us
    dot_general x1, matrix products, row_product(): lax.dot_general(shard_rows, value_rows, (((0,), (0,)), ((), ())), preferr...  12.6 us
    all_to_all x1, blocking collectives, local(): lax.all_to_all(key_out, 'seq', split_axis=0, concat_axis=1, tiled=True)  10.6 us
    all_to_all x2, local copies, waits for them, and re-layouts, local(): lax.all_to_all(out_grad[0], 'seq', split_axis=1, concat_axis=0, tiled=True)  8.58 us
  transfers between devices with their start and end apart: 8, of which 7 were waited for; matrix products, arithmetic and copies ran while one was open for 5% of the time, Pallas kernels for 11%

profile of v2, /device:TPU:8, one launch (start us, length us, event | category | flops | bytes accessed | tf_op | source)
XLA Modules:
  0.0 346.9 jit_solution(4086118132126252254)
XLA Ops:
  8.3 91.9 %collective-permute-done = bf16[128,8192]{1,0:T(8,128)(2,1)S(1)} collective-permute-done((bf16[128,8192]{1,0:T(8,128)(2,1)}, bf16[128,8192]{1,0:T(8,128)(2,1)S(1)}, u32[]{:S(2)}, u32[]{:S(2)}) %collective-permute-start) | collective-permute-done | bytes 2097184 | tf_op jit(solution)/shard_map/ppermute | solution.py:100
  100.2 4.0 %pad_maximum_fusion = bf16[256,8192]{1,0:T(8,128)(2,1)} fusion(bf16[128,8192]{1,0:T(8,128)(2,1)S(1)} %collective-permute-done, bf16[128,8192]{1,0:T(8,128)(2,1)} %bitcast.36), kind=kLoop, calls=%fused_computation.2 | loop fusion | flops 8388608 | bytes 8388608 | tf_op jit(solution)/shard_map/concatenate | solution.py:115
  106.1 3.7 %all-to-all-start.1 = ((bf16[128,4,256]{2,0,1:T(8,128)(2,1)}), bf16[128,4,256]{2,0,1:T(8,128)(2,1)S(1)}, u32[]{:S(2)}, u32[]{:S(2)}) async-start(bf16[128,4,256]{2,0,1:T(8,128)(2,1)} %copy.16), calls=%async_computation.1 | async-start | bytes 524288 | tf_op jit(solution)/shard_map/all_to_all | solution.py:103
  110.8 4.7 %all-to-all-done.1 = bf16[128,4,256]{2,0,1:T(8,128)(2,1)S(1)} async-done(((bf16[128,4,256]{2,0,1:T(8,128)(2,1)}), bf16[128,4,256]{2,0,1:T(8,128)(2,1)S(1)}, u32[]{:S(2)}, u32[]{:S(2)}) %all-to-all-start.1) | async-done | bytes 262176 | tf_op jit(solution)/shard_map/all_to_all | solution.py:103
  115.5 3.4 all-to-all-start.2
  118.9 3.5 %all_to_all.80 = bf16[128,4,2048]{2,1,0:T(4,128)(2,1)S(1)} reshape(bf16[1,128,8192]{2,1,0:T(8,128)(2,1)} %param.6) | data formatting | bytes 4194304 | tf_op jit(solution)/shard_map/all_to_all | solution.py:102
  122.5 2.5 copy.15
  124.9 2.6 all-to-all-done.2
  127.5 3.6 %all-to-all-start = ((bf16[128,4,2048]{2,0,1:T(8,128)(2,1)}), bf16[128,4,2048]{2,0,1:T(8,128)(2,1)S(1)}, u32[]{:S(2)}, u32[]{:S(2)}) async-start(bf16[128,4,2048]{2,0,1:T(8,128)(2,1)} %copy.15), calls=%async_computation | async-start | bytes 4194304 | tf_op jit(solution)/shard_map/all_to_all | solution.py:102
  131.2 4.5 %all_to_all.92 = bf16[128,4,2048]{2,1,0:T(4,128)(2,1)} reshape(bf16[1,128,8192]{2,1,0:T(8,128)(2,1)} %param.9) | data formatting | bytes 4194304 | tf_op jit(solution)/shard_map/all_to_all | solution.py:105
  135.7 4.1 %copy.18 = bf16[128,4,2048]{2,0,1:T(8,128)(2,1)} copy(bf16[128,4,2048]{2,1,0:T(4,128)(2,1)} %all_to_all.92) | data formatting | bytes 4194304 | tf_op jit(solution)/shard_map/all_to_all | solution.py:105
  139.7 39.2 %all-to-all-done = bf16[128,4,2048]{2,0,1:T(8,128)(2,1)S(1)} async-done(((bf16[128,4,2048]{2,0,1:T(8,128)(2,1)}), bf16[128,4,2048]{2,0,1:T(8,128)(2,1)S(1)}, u32[]{:S(2)}, u32[]{:S(2)}) %all-to-all-start) | async-done | bytes 2097184 | tf_op jit(solution)/shard_map/all_to_all | solution.py:102
  178.9 4.5 %all-to-all-start.3 = ((bf16[128,4,2048]{2,0,1:T(8,128)(2,1)}), bf16[128,4,2048]{2,0,1:T(8,128)(2,1)}, u32[]{:S(2)}, u32[]{:S(2)}) async-start(bf16[128,4,2048]{2,0,1:T(8,128)(2,1)} %copy.18), calls=%async_computation.3 | async-start | bytes 4194304 | tf_op jit(solution)/shard_map/all_to_all | solution.py:105
  183.4 32.3 %all-gather.doc_row_ref = s32[1,512]{1,0:T(1,128)S(1)} all-gather(s32[1,128]{1,0:T(1,128)S(1)} %copy-done.3), channel_id=2, replica_groups=mesh['section'=8,'seq'=4] {'seq'}, dimensions={1}, use_global_device_ids=true | all-gather | bytes 2560 | tf_op jit(solution)/shard_map/all_gather | solution.py:107
  215.8 36.9 %shard_map.85 = (bf16[512,2048]{1,0:T(8,128)(2,1)S(1)}, f32[512,256]{1,0:T(8,128)S(1)}, f32[512,256]{1,0:T(8,128)S(1)}) custom-call(bf16[512,2048]{1,0:T(8,128)(2,1)S(1)} %bitcast.29, bf16[512,256]{1,0:T(8,128)(2,1)S(1)} %bitcast.31, bf16[512,256]{1,0:T(8,128)(2,1)S(1)} %bitcast.32, bf16[512,2048]{1,0:T(8,128)(2,1)} %bitcast.7.grad_ref, ...), custom_call_target="tpu_custom_call" | custom-call | tf_op jit(solution)/shard_map/pallas_call | solution.py:61
  252.7 1.3 copy-done
  254.0 10.6 %all_to_all.108 = bf16[4,128,256]{2,1,0:T(8,128)(2,1)S(1)} all-to-all(bf16[4,128,256]{2,1,0:T(8,128)(2,1)S(1)} %bitcast.37), channel_id=1, replica_groups=mesh['section'=8,'seq'=4] {'seq'}, dimensions={0} | all-to-all | bytes 524288 | tf_op jit(solution)/shard_map/all_to_all | solution.py:113
  264.7 3.8 %all-to-all-start.4 = ((bf16[4,128,2048]{2,1,0:T(8,128)(2,1)}), bf16[4,128,2048]{2,1,0:T(8,128)(2,1)S(1)}, u32[]{:S(2)}, u32[]{:S(2)}) async-start(bf16[4,128,2048]{2,1,0:T(8,128)(2,1)} %bitcast.30), calls=%async_computation.4 | async-start | bytes 4194304 | tf_op jit(solution)/shard_map/all_to_all | solution.py:112
  269.7 7.5 %collective-permute-done.1 = bf16[512,256]{1,0:T(8,128)(2,1)S(1)} collective-permute-done((bf16[512,256]{1,0:T(8,128)(2,1)S(1)}, bf16[512,256]{1,0:T(8,128)(2,1)S(1)}, u32[]{:S(2)}, u32[]{:S(2)}) %collective-permute-start.1) | collective-permute-done | bytes 262176 | tf_op jit(solution)/shard_map/ppermute | solution.py:117
  277.2 38.5 %all-to-all-done.4 = bf16[4,128,2048]{2,1,0:T(8,128)(2,1)S(1)} async-done(((bf16[4,128,2048]{2,1,0:T(8,128)(2,1)}), bf16[4,128,2048]{2,1,0:T(8,128)(2,1)S(1)}, u32[]{:S(2)}, u32[]{:S(2)}) %all-to-all-start.4) | async-done | bytes 2097184 | tf_op jit(solution)/shard_map/all_to_all | solution.py:112
  315.7 3.0 copy.20
  318.6 4.4 %broadcast_in_dim.9 = bf16[1,128,8192]{2,1,0:T(8,128)(2,1)} reshape(bf16[128,4,2048]{2,1,0:T(4,128)(2,1)} %copy.20) | data formatting | bytes 4194304 | tf_op jit(solution)/shard_map/broadcast_in_dim | solution.py:125
  323.1 4.4 %all-gather.3.cloned.1.call-done = bf16[1024,8192]{1,0:T(8,128)(2,1)} async-done(((bf16[256,8192]{1,0:T(8,128)(2,1)}), bf16[1024,8192]{1,0:T(8,128)(2,1)}) %all-gather.3.cloned.1.call-update) | async-done | bytes 16777232 | tf_op jit(solution)/shard_map/all_gather | solution.py:116
  327.5 12.6 %fusion = bf16[1,8192,256]{2,1,0:T(8,128)(2,1)} fusion(bf16[1024,8192]{1,0:T(8,128)(2,1)} %all-gather.3.cloned.1.call-done, bf16[1024,256]{1,0:T(8,128)(2,1)S(1)} %bitcast.40), kind=kOutput, calls=%fused_computation.1 | convolution fusion | flops 4297064448 | bytes 21495808 | tf_op jit(solution)/shard_map/dot_general | solution.py:92
  (22 shorter events, 5.3 us)
Async XLA Ops:
  7.2 320.3 %all-gather.3.cloned.1.call-start = ((), (), s32[]{:S(2)}) async-start(), calls=%async_computation.6 | async-start | bytes 20971520 | tf_op jit(solution)/shard_map/all_gather | solution.py:116
  7.2 93.0 %collective-permute-start = (bf16[128,8192]{1,0:T(8,128)(2,1)}, bf16[128,8192]{1,0:T(8,128)(2,1)S(1)}, u32[]{:S(2)}, u32[]{:S(2)}) collective-permute-start(bf16[128,8192]{1,0:T(8,128)(2,1)} %bitcast.35), channel_id=1, source_target_pairs={{0,28},{4,24},{8,20},{12,16},{16,12},{20,8},{24,4},{28,0},{1,29},{... | collective-permute-start | bytes 6291464 | tf_op jit(solution)/shard_map/ppermute | solution.py:100
  104.3 0.9 copy-start.1
  104.3 5.6 %copy-start.2 = (bf16[1,128,1024]{2,1,0:T(8,128)(2,1)S(1)}, bf16[1,128,1024]{2,1,0:T(8,128)(2,1)}, u32[]{:S(2)}) copy-start(bf16[1,128,1024]{2,1,0:T(8,128)(2,1)} %param.8) | copy-start | bytes 786436
  106.1 9.4 %all-to-all-start.1 = ((bf16[128,4,256]{2,0,1:T(8,128)(2,1)}), bf16[128,4,256]{2,0,1:T(8,128)(2,1)S(1)}, u32[]{:S(2)}, u32[]{:S(2)}) async-start(bf16[128,4,256]{2,0,1:T(8,128)(2,1)} %copy.16), calls=%async_computation.1 | async-start | bytes 524288 | tf_op jit(solution)/shard_map/all_to_all | solution.py:103
  115.5 12.0 %all-to-all-start.2 = ((bf16[128,4,256]{2,0,1:T(8,128)(2,1)}), bf16[128,4,256]{2,0,1:T(8,128)(2,1)S(1)}, u32[]{:S(2)}, u32[]{:S(2)}) async-start(bf16[128,4,256]{2,0,1:T(8,128)(2,1)} %copy.17), calls=%async_computation.2 | async-start | bytes 524288 | tf_op jit(solution)/shard_map/all_to_all | solution.py:104
  127.5 51.4 %all-to-all-start = ((bf16[128,4,2048]{2,0,1:T(8,128)(2,1)}), bf16[128,4,2048]{2,0,1:T(8,128)(2,1)S(1)}, u32[]{:S(2)}, u32[]{:S(2)}) async-start(bf16[128,4,2048]{2,0,1:T(8,128)(2,1)} %copy.15), calls=%async_computation | async-start | bytes 4194304 | tf_op jit(solution)/shard_map/all_to_all | solution.py:102
  139.7 43.6 %copy-start.3 = (s32[1,128]{1,0:T(1,128)S(1)}, s32[1,128]{1,0:T(1,128)}, u32[]{:S(2)}) copy-start(s32[1,128]{1,0:T(1,128)} %param.11) | copy-start | bytes 1540
  178.9 36.9 %all-to-all-start.3 = ((bf16[128,4,2048]{2,0,1:T(8,128)(2,1)}), bf16[128,4,2048]{2,0,1:T(8,128)(2,1)}, u32[]{:S(2)}, u32[]{:S(2)}) async-start(bf16[128,4,2048]{2,0,1:T(8,128)(2,1)} %copy.18), calls=%async_computation.3 | async-start | bytes 4194304 | tf_op jit(solution)/shard_map/all_to_all | solution.py:105
  252.7 1.3 copy-start
  264.7 51.0 %all-to-all-start.4 = ((bf16[4,128,2048]{2,1,0:T(8,128)(2,1)}), bf16[4,128,2048]{2,1,0:T(8,128)(2,1)S(1)}, u32[]{:S(2)}, u32[]{:S(2)}) async-start(bf16[4,128,2048]{2,1,0:T(8,128)(2,1)} %bitcast.30), calls=%async_computation.4 | async-start | bytes 4194304 | tf_op jit(solution)/shard_map/all_to_all | solution.py:112
  268.5 8.6 %collective-permute-start.1 = (bf16[512,256]{1,0:T(8,128)(2,1)S(1)}, bf16[512,256]{1,0:T(8,128)(2,1)S(1)}, u32[]{:S(2)}, u32[]{:S(2)}) collective-permute-start(bf16[512,256]{1,0:T(8,128)(2,1)S(1)} %convert_element_type.10), channel_id=1, source_target_pairs={{0,28},{4,24},{8,20},{12,16},{16,12},{20,8},{24,4},{28,0},{1,29},{... | collective-permute-start | bytes 786440 | tf_op jit(solution)/shard_map/ppermute | solution.py:117
Sparse Core Ops, SparseCore 0:
  104.4 223.0 all-gather.2

commit v3 on v2

--- a/solution.py
+++ b/solution.py
@@ -49,42 +49,46 @@
                                           preferred_element_type=jnp.float32)
 
 
-def attention_grads(query_cols, key_cols, value_cols, grad_cols, doc_ids):
-    length = query_cols.shape[0]
-    kv_heads = key_cols.shape[1] // HEAD_WIDTH
-    q_heads = query_cols.shape[1] // HEAD_WIDTH
-    group_size = q_heads // kv_heads
+def attention_grads(merged, doc_ids, q_width, k_width):
+    length = merged.shape[0]
+    kv_heads = k_width // HEAD_WIDTH
+    group_size = q_width // k_width
     rows = min(length, 256)
     tiles = length // rows
-    head_block = lambda g, h, t: (t, g * group_size + h)
-    kv_block = lambda g, h, t: (0, g)
+    q_blocks, k_blocks = q_width // HEAD_WIDTH, k_width // HEAD_WIDTH
+
+    def head_at(base):
+        return pl.BlockSpec((rows, HEAD_WIDTH), lambda g, h, t: (t, base + g * group_size + h))
+
+    def kv_at(base):
+        return pl.BlockSpec((length, HEAD_WIDTH), lambda g, h, t: (0, base + g))
+
     query_out, key_acc, value_acc = pl.pallas_call(
         attention_kernel,
         grid=(kv_heads, group_size, tiles),
         in_specs=[
-            pl.BlockSpec((rows, HEAD_WIDTH), head_block),
-            pl.BlockSpec((length, HEAD_WIDTH), kv_block),
-            pl.BlockSpec((length, HEAD_WIDTH), kv_block),
-            pl.BlockSpec((rows, HEAD_WIDTH), head_block),
+            head_at(0),
+            kv_at(2 * q_blocks),
+            kv_at(2 * q_blocks + k_blocks),
+            head_at(q_blocks),
             pl.BlockSpec((rows, 1), lambda g, h, t: (t, 0)),
             pl.BlockSpec((1, length), lambda g, h, t: (0, 0)),
         ],
         out_specs=[
-            pl.BlockSpec((rows, HEAD_WIDTH), head_block),
-            pl.BlockSpec((length, HEAD_WIDTH), kv_block),
-            pl.BlockSpec((length, HEAD_WIDTH), kv_block),
+            pl.BlockSpec((rows, HEAD_WIDTH), lambda g, h, t: (t, g * group_size + h)),
+            kv_at(0),
+            kv_at(0),
         ],
         out_shape=[
-            jax.ShapeDtypeStruct(query_cols.shape, jnp.bfloat16),
-            jax.ShapeDtypeStruct(key_cols.shape, jnp.float32),
-            jax.ShapeDtypeStruct(value_cols.shape, jnp.float32),
+            jax.ShapeDtypeStruct((length, q_width), jnp.bfloat16),
+            jax.ShapeDtypeStruct((length, k_width), jnp.float32),
+            jax.ShapeDtypeStruct((length, k_width), jnp.float32),
         ],
         compiler_params=pltpu.CompilerParams(
             dimension_semantics=("arbitrary", "arbitrary", "arbitrary"),
             vmem_limit_bytes=48 * 1024 * 1024,
         ),
-    )(query_cols, key_cols, value_cols, grad_cols, doc_ids.reshape(length, 1),
-      doc_ids.reshape(1, length))
+    )(merged, merged, merged, merged, doc_ids.reshape(length, 1), doc_ids.reshape(1, length))
     return (query_out, key_acc.astype(jnp.bfloat16), value_acc.astype(jnp.bfloat16))
 
 
@@ -96,32 +100,35 @@
 
 def local(queries, key_states, section_value_states, out_grad, layer_input, doc_segments):
     section_count = lax.axis_size("section")
+    seq_count = lax.axis_size("seq")
     mirror = [(i, section_count - 1 - i) for i in range(section_count)]
-    mirror_rows = lax.ppermute(layer_input[0], "section", mirror)
-    query_head, key_head, value_head, grad_head = (
-        lax.all_to_all(queries[0], "seq", split_axis=1, concat_axis=0, tiled=True),
-        lax.all_to_all(key_states[0], "seq", split_axis=1, concat_axis=0, tiled=True),
-        lax.all_to_all(section_value_states[0], "seq", split_axis=1, concat_axis=0, tiled=True),
-        lax.all_to_all(out_grad[0], "seq", split_axis=1, concat_axis=0, tiled=True),
-    )
-    doc_ids = lax.all_gather(doc_segments[0], "seq", axis=0, tiled=True)
-    query_out, key_out, value_out = attention_grads(
-        query_head, key_head, value_head, grad_head, doc_ids
-    )
+    own_rows = layer_input[0]
+    own_gathered = lax.all_gather(own_rows, "seq", axis=0, tiled=True)
+    mirror_rows = lax.ppermute(own_rows, "section", mirror)
+    mirror_gathered = lax.all_gather(mirror_rows, "seq", axis=0, tiled=True)
+    positions = queries.shape[1]
+    q_width = queries.shape[2] // seq_count
+    k_width = key_states.shape[2] // seq_count
+    parts = [
+        queries[0].reshape(positions, seq_count, q_width),
+        out_grad[0].reshape(positions, seq_count, q_width),
+        key_states[0].reshape(positions, seq_count, k_width),
+        section_value_states[0].reshape(positions, seq_count, k_width),
+    ]
+    merged = lax.all_to_all(
+        jnp.concatenate(parts, axis=2), "seq", split_axis=1, concat_axis=0, tiled=True
+    ).reshape(positions * seq_count, 2 * q_width + 2 * k_width)
+    doc_ids = lax.all_to_all(
+        jnp.broadcast_to(doc_segments, (seq_count, positions)), "seq",
+        split_axis=0, concat_axis=0, tiled=True,
+    ).reshape(seq_count * positions)
+    query_out, key_out, value_out = attention_grads(merged, doc_ids, q_width, k_width)
     query_back, key_back = (
         lax.all_to_all(query_out, "seq", split_axis=0, concat_axis=1, tiled=True),
         lax.all_to_all(key_out, "seq", split_axis=0, concat_axis=1, tiled=True),
     )
-    both_rows = jnp.concatenate([layer_input[0], mirror_rows], axis=0)
-    gathered = lax.all_gather(both_rows, "seq", axis=0, tiled=True)
     mirror_value = lax.ppermute(value_out, "section", mirror)
-    seq_count = lax.axis_size("seq")
-    chunk = value_out.shape[0] // seq_count
-    both_values = jnp.stack(
-        [value_out.reshape(seq_count, chunk, -1), mirror_value.reshape(seq_count, chunk, -1)],
-        axis=1,
-    ).reshape(2 * value_out.shape[0], value_out.shape[1])
-    paired = row_product(gathered, both_values)
+    paired = row_product(own_gathered, value_out) + row_product(mirror_gathered, mirror_value)
     return (query_back[None], key_back[None], paired.astype(jnp.bfloat16)[None])
 
 

time: 348 us -> 320 us (0.920)
  blocking collectives: 42.9 us -> 11.3 us
  matrix products: 12.6 us -> 19.1 us
  starting transfers between devices: 20.2 us -> 13.7 us
    all_gather x1 -> x0, blocking collectives: 32.3 us -> none  [local(): doc_ids = lax.all_gather(doc_segments[0], 'seq', axis=0, tiled=True)]
    all_to_all x4 -> x2, waiting for transfers between devices: 46.5 us -> 75.6 us  [the longest x1 75.6 us: local(): lax.all_to_all(jnp.concatenate(parts, axis=2), 'seq', split_axis=1, conca...]
    all_to_all x8 -> x0, local copies, waits for them, and re-layouts: 16.4 us -> none  [the longest x2 8.58 us: local(): lax.all_to_all(out_grad[0], 'seq', split_axis=1, concat_axis=0, tiled=True)]
    all_to_all x1, waiting for transfers between devices: 38.5 us -> 23.1 us  [local(): lax.all_to_all(query_out, 'seq', split_axis=0, concat_axis=1, tiled=True)]
    another operation x0 -> x9, local copies, waits for them, and re-layouts: none -> 11.8 us  [the longest x2 5.79 us: local(): queries[0].reshape(positions, seq_count, q_width)]
    ppermute x1, waiting for transfers between devices: 7.45 us -> 0.01 us  [local(): mirror_value = lax.ppermute(value_out, 'section', mirror)]
    dot_general x1 -> x2, matrix products: 12.6 us -> 19.1 us  [row_product(): lax.dot_general(shard_rows, value_rows, (((0,), (0,)), ((), ())), preferr...]
    all_to_all x4 -> x2, starting transfers between devices: 15.2 us -> 8.68 us  [the longest x1 4.96 us: local(): lax.all_to_all(jnp.concatenate(parts, axis=2), 'seq', split_axis=1, conca...]
  transfers between devices with their start and end apart: 8 -> 7, of which waited for: 7 -> 3; matrix products, arithmetic and copies ran while one was open for 5% -> 10% of each run, Pallas kernels for 11% -> 12%
where the time goes in v3:
time: 320 us; the launch traced here: 319 us
  waiting for transfers between devices  191 us (60%)
  Pallas kernels  37.6 us (12%)
  local copies, waits for them, and re-layouts  29.6 us (9%)
  matrix products  19.1 us (6%)
  between operations  14.2 us (4%)
  starting transfers between devices  13.7 us (4%)
  blocking collectives  11.3 us (4%)
    ppermute x1, waiting for transfers between devices, local(): mirror_rows = lax.ppermute(own_rows, 'section', mirror)  91.9 us
    all_to_all x1, waiting for transfers between devices, local(): lax.all_to_all(jnp.concatenate(parts, axis=2), 'seq', split_axis=1, conca...  75.6 us
    pallas_call x1, Pallas kernels, attention_grads(): pl.pallas_call(attention_kernel, grid=(kv_heads, group_size, tiles), in_s...  37.6 us
    all_to_all x1, waiting for transfers between devices, local(): lax.all_to_all(query_out, 'seq', split_axis=0, concat_axis=1, tiled=True)  23.1 us
    dot_general x2, matrix products, row_product(): lax.dot_general(shard_rows, value_rows, (((0,), (0,)), ((), ())), preferr...  19.1 us
    all_to_all x1, blocking collectives, local(): lax.all_to_all(key_out, 'seq', split_axis=0, concat_axis=1, tiled=True)  11.3 us
    unnamed x7, local copies, waits for them, and re-layouts  8.11 us
  transfers between devices with their start and end apart: 7, of which 3 were waited for; matrix products, arithmetic and copies ran while one was open for 10% of the time, Pallas kernels for 12%

profile of v3, /device:TPU:8, one launch (start us, length us, event | category | flops | bytes accessed | tf_op | source)
XLA Modules:
  0.0 319.2 jit_solution(6030402467900772419)
XLA Ops:
  7.2 0.7 all-gather.6.cloned.1.call-update
  8.0 1.1 collective-permute-start.1
  9.0 91.9 %collective-permute-done.1 = bf16[128,8192]{1,0:T(8,128)(2,1)S(1)} collective-permute-done((bf16[128,8192]{1,0:T(8,128)(2,1)}, bf16[128,8192]{1,0:T(8,128)(2,1)S(1)}, u32[]{:S(2)}, u32[]{:S(2)}) %collective-permute-start.1) | collective-permute-done | bytes 2097184 | tf_op jit(solution)/shard_map/ppermute | solution.py:107
  101.0 1.3 copy-done.1
  102.3 1.2 broadcast_in_dim.14
  103.6 3.7 %all-to-all-start.1 = ((s32[4,1,128]{2,1,0:T(1,128)}), s32[4,1,128]{2,1,0:T(1,128)S(1)}, u32[]{:S(2)}, u32[]{:S(2)}) async-start(s32[4,1,128]{2,1,0:T(1,128)} %broadcast_in_dim.14), calls=%async_computation.1 | async-start | bytes 4096 | tf_op jit(solution)/shard_map/all_to_all | solution.py:121
  107.3 1.1 reshape_squeeze.14
  108.7 3.3 %reshape_squeeze.12 = bf16[128,4,2048]{2,1,0:T(4,128)(2,1)S(1)} reshape(bf16[1,128,8192]{2,1,0:T(8,128)(2,1)} %param.6) | data formatting | bytes 4194304 | tf_op jit(solution)/shard_map/reshape;squeeze | solution.py:113
  112.0 2.5 copy.24
  114.5 3.3 %reshape_squeeze.13 = bf16[128,4,2048]{2,1,0:T(4,128)(2,1)S(1)} reshape(bf16[1,128,8192]{2,1,0:T(8,128)(2,1)} %param.9) | data formatting | bytes 4194304 | tf_op jit(solution)/shard_map/reshape;squeeze | solution.py:114
  117.8 1.2 copy.25
  119.4 2.3 pad_maximum_fusion
  121.7 5.0 %all-to-all-start = ((bf16[128,4,4608]{2,0,1:T(8,128)(2,1)}), bf16[128,4,4608]{2,0,1:T(8,128)(2,1)}, u32[]{:S(2)}, u32[]{:S(2)}) async-start(bf16[128,4,4608]{2,0,1:T(8,128)(2,1)} %pad_maximum_fusion), calls=%async_computation | async-start | bytes 9437184 | tf_op jit(solution)/shard_map/all_to_all | solution.py:118
  126.9 75.6 %all-to-all-done = bf16[128,4,4608]{2,0,1:T(8,128)(2,1)} async-done(((bf16[128,4,4608]{2,0,1:T(8,128)(2,1)}), bf16[128,4,4608]{2,0,1:T(8,128)(2,1)}, u32[]{:S(2)}, u32[]{:S(2)}) %all-to-all-start) | async-done | bytes 4718624 | tf_op jit(solution)/shard_map/all_to_all | solution.py:118
  202.5 37.6 %shard_map.88 = (bf16[512,2048]{1,0:T(8,128)(2,1)}, f32[512,256]{1,0:T(8,128)S(1)}, f32[512,256]{1,0:T(8,128)S(1)}) custom-call(bf16[512,4608]{1,0:T(8,128)(2,1)} %bitcast.2.query_ref.key_ref.value_ref.grad_ref, bf16[512,4608]{1,0:T(8,128)(2,1)} %bitcast.2.query_ref.key_ref.value_ref.grad_ref, bf16[512,4608]{1,0:T(8,128)(2,1)} %bitcast.2.query_ref.key_ref.value_ref.grad_ref, ...), custom_call_target="tpu_custom_call" | custom-call | tf_op jit(solution)/shard_map/pallas_call | solution.py:66
  240.1 11.3 %all_to_all.53 = bf16[4,128,256]{2,1,0:T(8,128)(2,1)S(1)} all-to-all(bf16[4,128,256]{2,1,0:T(8,128)(2,1)S(1)} %bitcast.27), channel_id=1, replica_groups=mesh['section'=8,'seq'=4] {'seq'}, dimensions={0} | all-to-all | bytes 524288 | tf_op jit(solution)/shard_map/all_to_all | solution.py:128
  251.4 3.8 %all-to-all-start.2 = ((bf16[4,128,2048]{2,1,0:T(8,128)(2,1)}), bf16[4,128,2048]{2,1,0:T(8,128)(2,1)S(1)}, u32[]{:S(2)}, u32[]{:S(2)}) async-start(bf16[4,128,2048]{2,1,0:T(8,128)(2,1)} %bitcast.6), calls=%async_computation.2 | async-start | bytes 4194304 | tf_op jit(solution)/shard_map/all_to_all | solution.py:127
  255.5 0.9 broadcast_in_dim.16
  256.4 23.1 %all-to-all-done.2 = bf16[4,128,2048]{2,1,0:T(8,128)(2,1)S(1)} async-done(((bf16[4,128,2048]{2,1,0:T(8,128)(2,1)}), bf16[4,128,2048]{2,1,0:T(8,128)(2,1)S(1)}, u32[]{:S(2)}, u32[]{:S(2)}) %all-to-all-start.2) | async-done | bytes 2097184 | tf_op jit(solution)/shard_map/all_to_all | solution.py:127
  279.5 2.9 copy.29
  282.4 4.4 %broadcast_in_dim.15 = bf16[1,128,8192]{2,1,0:T(8,128)(2,1)} reshape(bf16[128,4,2048]{2,1,0:T(4,128)(2,1)} %copy.29) | data formatting | bytes 4194304 | tf_op jit(solution)/shard_map/broadcast_in_dim | solution.py:132
  286.9 9.0 %fusion.2 = f32[256,8192]{1,0:T(8,128)} fusion(bf16[512,256]{1,0:T(8,128)(2,1)S(1)} %convert_element_type.13, bf16[1,512,8192]{2,1,0:T(8,128)(2,1)} %all-gather.6.cloned.1.call-done), kind=kOutput, calls=%fused_computation.3 | convolution fusion | flops 2147483648 | bytes 17039360 | tf_op jit(solution)/shard_map/dot_general | solution.py:96
  295.9 10.2 %fusion.1 = bf16[1,8192,256]{1,2,0:T(8,128)(2,1)} fusion(f32[256,8192]{1,0:T(8,128)} %fusion.2, bf16[512,256]{1,0:T(8,128)(2,1)S(1)} %collective-permute-done, bf16[512,8192]{1,0:T(8,128)(2,1)} %all-gather.4.cloned.1.call-done), kind=kOutput, calls=%fused_computation.2 | convolution fusion | flops 2151677952 | bytes 21233664 | tf_op jit(solution)/shard_map/dot_general | solution.py:96
  306.0 6.4 %copy.31 = bf16[1,8192,256]{2,1,0:T(8,128)(2,1)} copy(bf16[1,8192,256]{1,2,0:T(8,128)(2,1)} %fusion.1) | data formatting | bytes 8388608
  (20 shorter events, 1.2 us)
Async XLA Ops:
  7.2 101.3 %copy-start.2 = (bf16[1,128,1024]{2,1,0:T(8,128)(2,1)S(1)}, bf16[1,128,1024]{2,1,0:T(8,128)(2,1)}, u32[]{:S(2)}) copy-start(bf16[1,128,1024]{2,1,0:T(8,128)(2,1)} %param.8) | copy-start | bytes 786436
  7.2 279.7 %all-gather.6.cloned.1.call-start = ((), (), s32[]{:S(2)}) async-start(), calls=%async_computation.5 | async-start | bytes 10485760 | tf_op jit(solution)/shard_map/all_gather | solution.py:106
  7.9 287.9 %all-gather.4.cloned.1.call-start = ((), (), s32[]{:S(2)}) async-start(), calls=%async_computation.4 | async-start | bytes 10485760 | tf_op jit(solution)/shard_map/all_gather | solution.py:108
  8.0 93.0 %collective-permute-start.1 = (bf16[128,8192]{1,0:T(8,128)(2,1)}, bf16[128,8192]{1,0:T(8,128)(2,1)S(1)}, u32[]{:S(2)}, u32[]{:S(2)}) collective-permute-start(bf16[128,8192]{1,0:T(8,128)(2,1)} %bitcast.26), channel_id=1, source_target_pairs={{0,28},{4,24},{8,20},{12,16},{16,12},{20,8},{24,4},{28,0},{1,29},{... | collective-permute-start | bytes 6291464 | tf_op jit(solution)/shard_map/ppermute | solution.py:107
  101.0 1.3 copy-start.1
  103.6 18.2 %all-to-all-start.1 = ((s32[4,1,128]{2,1,0:T(1,128)}), s32[4,1,128]{2,1,0:T(1,128)S(1)}, u32[]{:S(2)}, u32[]{:S(2)}) async-start(s32[4,1,128]{2,1,0:T(1,128)} %broadcast_in_dim.14), calls=%async_computation.1 | async-start | bytes 4096 | tf_op jit(solution)/shard_map/all_to_all | solution.py:121
  117.8 1.6 copy-start
  121.7 80.7 %all-to-all-start = ((bf16[128,4,4608]{2,0,1:T(8,128)(2,1)}), bf16[128,4,4608]{2,0,1:T(8,128)(2,1)}, u32[]{:S(2)}, u32[]{:S(2)}) async-start(bf16[128,4,4608]{2,0,1:T(8,128)(2,1)} %pad_maximum_fusion), calls=%async_computation | async-start | bytes 9437184 | tf_op jit(solution)/shard_map/all_to_all | solution.py:118
  251.4 28.1 %all-to-all-start.2 = ((bf16[4,128,2048]{2,1,0:T(8,128)(2,1)}), bf16[4,128,2048]{2,1,0:T(8,128)(2,1)S(1)}, u32[]{:S(2)}, u32[]{:S(2)}) async-start(bf16[4,128,2048]{2,1,0:T(8,128)(2,1)} %bitcast.6), calls=%async_computation.2 | async-start | bytes 4194304 | tf_op jit(solution)/shard_map/all_to_all | solution.py:127
  255.2 40.6 %collective-permute-start = (bf16[512,256]{1,0:T(8,128)(2,1)S(1)}, bf16[512,256]{1,0:T(8,128)(2,1)S(1)}, u32[]{:S(2)}, u32[]{:S(2)}) collective-permute-start(bf16[512,256]{1,0:T(8,128)(2,1)S(1)} %convert_element_type.13), channel_id=1, source_target_pairs={{0,28},{4,24},{8,20},{12,16},{16,12},{20,8},{24,4},{28,0},{1,29},{... | collective-permute-start | bytes 786440 | tf_op jit(solution)/shard_map/ppermute | solution.py:130
Sparse Core Ops, SparseCore 0:
  9.8 88.6 all-gather.5
  102.4 155.4 all-gather.3
